TPU v7x, 32 devices: a whole 2x2x4 slice. The times are simulated.
32 devices in a mesh: starts: 2 (over y), gx: 8 (over z, x), gy: 2 (over core).
Axes of the slice: x: 2, y: 2, z: 4, core: 2. Of those that a mesh axis runs over, the one named last changes fastest.
Arguments:
- chi_final: float32 [2, 64, 128, 256], P(None, ('starts', 'gx'), 'gy'), parts along dimension 1, may hold values from -30 to 30
- psi_late: float32 [2, 64, 128, 256], P(None, ('starts', 'gx'), 'gy'), parts along dimension 1, may hold values from -0.7 to 0.7
- psi_early: float32 [2, 64, 128, 256], P(None, ('starts', 'gx'), 'gy'), parts along dimension 1, may hold values from -0.7 to 0.7
- trap: float32 [32, 128, 256], P('gx', 'gy'), may hold values from 0 to 1
- controls: float32 [4, 64, 256], P('starts', 'gy'), parts along dimension 0, may hold values from -0.5 to 0.5
Outputs:
- chi_start: float32 [2, 64, 128, 256], P(None, ('starts', 'gx'), 'gy'), parts along dimension 1
- grad_rows: float32 [4, 64, 256], P('starts', 'gy'), parts along dimension 0
- adjoint_power: float32 [2], P('starts'), parts along dimension 0
There are 2 independent parts, one for each index of `starts`. A program takes and returns all parts, laid end to end along the dimension named above; an argument that names none is the same for every part. Nothing has to cross between parts.
All inputs are finite; a program needn't handle non-finite values.
Results may differ from a plain program's by a relative error of at most 0.0005.
Values sent between devices are 32-bit elements; how exact they have to be, the bound alone decides.
No kernel may reach another device: no remote copies, remote signals or barrier semaphores. Data moves between devices by JAX's collectives and lax.ppermute only.
A program may use at most 64 MiB of HBM per device.

v0:
```python
import math
import jax
import jax.numpy as jnp
from jax import lax
from jax.sharding import PartitionSpec as P

COUPLING = 1.0
STEP_SIZE = 0.2


def extended(block, sides, width):
    for axis, dim in sides:
        count = lax.axis_size(axis)
        forward = [(i, i + 1) for i in range(count - 1)]
        backward = [(target, source) for source, target in forward]
        low = lax.ppermute(
            lax.slice_in_dim(block, block.shape[dim] - width, None, axis=dim), axis, forward
        )
        high = lax.ppermute(lax.slice_in_dim(block, 0, width, axis=dim), axis, backward)
        block = jnp.concatenate([low, block, high], axis=dim)
    return block


def coefficients(psi, trap, control, profile):
    real_part = psi[0]
    imag_part = psi[1]
    fine_control = jnp.repeat(control, 2, axis=0)
    potential = trap + profile[:, None, None] * fine_control[None, :, :]
    weight = potential + 2.0 * COUPLING * (real_part * real_part + imag_part * imag_part)
    mix_a = COUPLING * (real_part * real_part - imag_part * imag_part)
    mix_b = 2.0 * COUPLING * real_part * imag_part
    return (weight, mix_a, mix_b)


def apply_coef(lapl, field, coef):
    weight, mix_a, mix_b = coef
    real_part = field[0]
    imag_part = field[1]
    upper = -0.5 * lapl[0] + (weight + mix_a) * real_part + mix_b * imag_part
    lower = -0.5 * lapl[1] + mix_b * real_part + (weight - mix_a) * imag_part
    return jnp.stack([-lower, upper])


def operator(field, coef):
    padded = extended(field, (("gx", 1), ("gy", 2)), 1)
    z_padded = jnp.pad(field, ((0, 0), (0, 0), (0, 0), (1, 1)))
    total = padded[:, 2:, 1:-1, :] + padded[:, :-2, 1:-1, :]
    total = total + padded[:, 1:-1, 2:, :] + padded[:, 1:-1, :-2, :]
    total = total + z_padded[:, :, :, 2:] + z_padded[:, :, :, :-2]
    lapl = total - 6.0 * field
    return apply_coef(lapl, field, coef)


def rk_step(field, coef):
    section_one = operator(field, coef)
    section_two = operator(field + 0.5 * STEP_SIZE * section_one, coef)
    section_three = operator(field + 0.5 * STEP_SIZE * section_two, coef)
    section_four = operator(field + STEP_SIZE * section_three, coef)
    return field + STEP_SIZE / 6.0 * (
        section_one + 2.0 * section_two + 2.0 * section_three + section_four
    )


def row_terms(field, psi, profile):
    intersection = field[0] * psi[1] - field[1] * psi[0]
    summed = jnp.sum(intersection * profile[:, None, None], axis=0)
    return summed.reshape(summed.shape[0] // 2, 2, summed.shape[1]).sum(axis=1)


def on_device(chi_final, psi_late, psi_early, trap, controls):
    planes = chi_final.shape[1]
    width_y = chi_final.shape[2]
    depth = chi_final.shape[3]
    total_x = planes * lax.axis_size("gx")
    total_y = width_y * lax.axis_size("gy")
    first = lax.axis_index("gx") * planes
    x_index = (first + jnp.arange(planes, dtype=jnp.int32)).astype(jnp.float32)
    profile = 1.0 + 0.5 * jnp.cos(2.0 * math.pi * x_index / float(total_x))
    coef_late = coefficients(psi_late, trap, controls[1], profile)
    coef_early = coefficients(psi_early, trap, controls[0], profile)
    chi_late = rk_step(chi_final, coef_late)
    chi_start = rk_step(chi_late, coef_early)
    rows = jnp.stack(
        [row_terms(chi_start, psi_early, profile), row_terms(chi_late, psi_late, profile)]
    )
    local_sq = jnp.sum(chi_start * chi_start)
    squares = lax.psum(local_sq, ("gx", "gy"))
    rows_sum = lax.psum(rows, "gx")
    power = squares / float(total_x * total_y * depth)
    grad_rows = rows_sum / jnp.sqrt(float(total_x) * (power + 1e-06))
    return (chi_start, grad_rows, jnp.reshape(power, (1,)))


def solution(mesh):
    placed = (
        P(None, ("starts", "gx"), "gy", None),
        P(None, ("starts", "gx"), "gy", None),
        P(None, ("starts", "gx"), "gy", None),
        P("gx", "gy", None),
        P("starts", "gy", None),
    )
    return jax.shard_map(
        on_device,
        mesh=mesh,
        in_specs=placed,
        out_specs=(P(None, ("starts", "gx"), "gy", None), P("starts", "gy", None), P("starts")),
        check_vma=False,
    )
```

profile of v0, /device:TPU:0, one launch (start us, length us, event | category | flops | bytes accessed | tf_op | source)
XLA Modules:
  0.0 232.7 jit_solution(15009674649921705698)
XLA Ops:
  9.6 5.5 %collective-permute-start.1 = (f32[2,1,64,256]{3,2,1,0:T(8,128)S(1)}, f32[2,1,64,256]{3,2,1,0:T(8,128)S(1)}, u32[]{:S(2)}, u32[]{:S(2)}) collective-permute-start(f32[2,1,64,256]{3,2,1,0:T(8,128)S(1)} %get-tuple-element.62), channel_id=1, source_target_pairs={{0,2},{2,4},{4,6},{6,8},{8,10},{10,12},{12,14},{1,3},{3,5},{5,7},{... | collective-permute-start | bytes 393224 | tf_op jit(solution)/shard_map/ppermute | solution.py:16
  16.5 3.1 %collective-permute-done.1 = f32[2,1,64,256]{3,2,1,0:T(8,128)S(1)} collective-permute-done((f32[2,1,64,256]{3,2,1,0:T(8,128)S(1)}, f32[2,1,64,256]{3,2,1,0:T(8,128)S(1)}, u32[]{:S(2)}, u32[]{:S(2)}) %collective-permute-start.1) | collective-permute-done | bytes 131104 | tf_op jit(solution)/shard_map/ppermute | solution.py:16
  21.0 3.0 %collective-permute-start.3 = (f32[2,6,1,256]{3,2,1,0:T(1,128)S(1)}, f32[2,6,1,256]{3,2,1,0:T(1,128)S(1)}, u32[]{:S(2)}, u32[]{:S(2)}) collective-permute-start(f32[2,6,1,256]{3,2,1,0:T(1,128)S(1)} %get-tuple-element.46), channel_id=1, source_target_pairs={{0,1},{2,3},{4,5},{6,7},{8,9},{10,11},{12,13},{14,15},{16,17},{18,... | collective-permute-start | bytes 36872 | tf_op jit(solution)/shard_map/ppermute | solution.py:16
  25.7 4.4 %collective-permute-start.5 = (f32[2,1,64,256]{3,2,1,0:T(8,128)S(1)}, f32[2,1,64,256]{3,2,1,0:T(8,128)S(1)}, u32[]{:S(2)}, u32[]{:S(2)}) collective-permute-start(f32[2,1,64,256]{3,2,1,0:T(8,128)S(1)} %get-tuple-element.59), channel_id=1, source_target_pairs={{0,2},{2,4},{4,6},{6,8},{8,10},{10,12},{12,14},{1,3},{3,5},{5,7},{... | collective-permute-start | bytes 393224 | tf_op jit(solution)/shard_map/ppermute | solution.py:16
  33.3 4.1 %collective-permute-done.4 = f32[2,1,64,256]{3,2,1,0:T(8,128)S(1)} collective-permute-done((f32[2,1,64,256]{3,2,1,0:T(8,128)S(1)}, f32[2,1,64,256]{3,2,1,0:T(8,128)S(1)}, u32[]{:S(2)}, u32[]{:S(2)}) %collective-permute-start.4) | collective-permute-done | bytes 131104 | tf_op jit(solution)/shard_map/ppermute | solution.py:19
  38.8 3.0 %collective-permute-start.7 = (f32[2,6,1,256]{3,2,1,0:T(1,128)S(1)}, f32[2,6,1,256]{3,2,1,0:T(1,128)S(1)}, u32[]{:S(2)}, u32[]{:S(2)}) collective-permute-start(f32[2,6,1,256]{3,2,1,0:T(1,128)S(1)} %get-tuple-element.44), channel_id=1, source_target_pairs={{0,1},{2,3},{4,5},{6,7},{8,9},{10,11},{12,13},{14,15},{16,17},{18,... | collective-permute-start | bytes 36872 | tf_op jit(solution)/shard_map/ppermute | solution.py:16
  43.3 4.5 %collective-permute-start.9 = (f32[2,1,64,256]{3,2,1,0:T(8,128)S(1)}, f32[2,1,64,256]{3,2,1,0:T(8,128)S(1)}, u32[]{:S(2)}, u32[]{:S(2)}) collective-permute-start(f32[2,1,64,256]{3,2,1,0:T(8,128)S(1)} %get-tuple-element.57), channel_id=1, source_target_pairs={{0,2},{2,4},{4,6},{6,8},{8,10},{10,12},{12,14},{1,3},{3,5},{5,7},{... | collective-permute-start | bytes 393224 | tf_op jit(solution)/shard_map/ppermute | solution.py:16
  51.1 4.1 %collective-permute-done.8 = f32[2,1,64,256]{3,2,1,0:T(8,128)S(1)} collective-permute-done((f32[2,1,64,256]{3,2,1,0:T(8,128)S(1)}, f32[2,1,64,256]{3,2,1,0:T(8,128)S(1)}, u32[]{:S(2)}, u32[]{:S(2)}) %collective-permute-start.8) | collective-permute-done | bytes 131104 | tf_op jit(solution)/shard_map/ppermute | solution.py:19
  56.5 3.0 %collective-permute-start.11 = (f32[2,6,1,256]{3,2,1,0:T(1,128)S(1)}, f32[2,6,1,256]{3,2,1,0:T(1,128)S(1)}, u32[]{:S(2)}, u32[]{:S(2)}) collective-permute-start(f32[2,6,1,256]{3,2,1,0:T(1,128)S(1)} %get-tuple-element.42), channel_id=1, source_target_pairs={{0,1},{2,3},{4,5},{6,7},{8,9},{10,11},{12,13},{14,15},{16,17},{18,... | collective-permute-start | bytes 36872 | tf_op jit(solution)/shard_map/ppermute | solution.py:16
  61.0 4.0 %collective-permute-start.13 = (f32[2,1,64,256]{3,2,1,0:T(8,128)S(1)}, f32[2,1,64,256]{3,2,1,0:T(8,128)S(1)}, u32[]{:S(2)}, u32[]{:S(2)}) collective-permute-start(f32[2,1,64,256]{3,2,1,0:T(8,128)S(1)} %get-tuple-element.55), channel_id=1, source_target_pairs={{0,2},{2,4},{4,6},{6,8},{8,10},{10,12},{12,14},{1,3},{3,5},{5,7},{... | collective-permute-start | bytes 393224 | tf_op jit(solution)/shard_map/ppermute | solution.py:16
  68.2 4.1 %collective-permute-done.12 = f32[2,1,64,256]{3,2,1,0:T(8,128)S(1)} collective-permute-done((f32[2,1,64,256]{3,2,1,0:T(8,128)S(1)}, f32[2,1,64,256]{3,2,1,0:T(8,128)S(1)}, u32[]{:S(2)}, u32[]{:S(2)}) %collective-permute-start.12) | collective-permute-done | bytes 131104 | tf_op jit(solution)/shard_map/ppermute | solution.py:19
  73.7 3.0 %collective-permute-start.15 = (f32[2,6,1,256]{3,2,1,0:T(1,128)S(1)}, f32[2,6,1,256]{3,2,1,0:T(1,128)S(1)}, u32[]{:S(2)}, u32[]{:S(2)}) collective-permute-start(f32[2,6,1,256]{3,2,1,0:T(1,128)S(1)} %get-tuple-element.40), channel_id=1, source_target_pairs={{0,1},{2,3},{4,5},{6,7},{8,9},{10,11},{12,13},{14,15},{16,17},{18,... | collective-permute-start | bytes 36872 | tf_op jit(solution)/shard_map/ppermute | solution.py:16
  78.2 4.0 %collective-permute-start.17 = (f32[2,1,64,256]{3,2,1,0:T(8,128)S(1)}, f32[2,1,64,256]{3,2,1,0:T(8,128)S(1)}, u32[]{:S(2)}, u32[]{:S(2)}) collective-permute-start(f32[2,1,64,256]{3,2,1,0:T(8,128)S(1)} %get-tuple-element.53), channel_id=1, source_target_pairs={{0,2},{2,4},{4,6},{6,8},{8,10},{10,12},{12,14},{1,3},{3,5},{5,7},{... | collective-permute-start | bytes 393224 | tf_op jit(solution)/shard_map/ppermute | solution.py:16
  85.5 4.1 %collective-permute-done.16 = f32[2,1,64,256]{3,2,1,0:T(8,128)S(1)} collective-permute-done((f32[2,1,64,256]{3,2,1,0:T(8,128)S(1)}, f32[2,1,64,256]{3,2,1,0:T(8,128)S(1)}, u32[]{:S(2)}, u32[]{:S(2)}) %collective-permute-start.16) | collective-permute-done | bytes 131104 | tf_op jit(solution)/shard_map/ppermute | solution.py:19
  91.6 4.2 %collective-permute-start.19 = (f32[2,6,1,256]{3,2,1,0:T(1,128)S(1)}, f32[2,6,1,256]{3,2,1,0:T(1,128)}, u32[]{:S(2)}, u32[]{:S(2)}) collective-permute-start(f32[2,6,1,256]{3,2,1,0:T(1,128)S(1)} %get-tuple-element.38), channel_id=1, source_target_pairs={{0,1},{2,3},{4,5},{6,7},{8,9},{10,11},{12,13},{14,15},{16,17},{18,... | collective-permute-start | bytes 36872 | tf_op jit(solution)/shard_map/ppermute | solution.py:16
  100.0 4.0 %collective-permute-start.21 = (f32[2,1,64,256]{3,2,1,0:T(8,128)S(1)}, f32[2,1,64,256]{3,2,1,0:T(8,128)S(1)}, u32[]{:S(2)}, u32[]{:S(2)}) collective-permute-start(f32[2,1,64,256]{3,2,1,0:T(8,128)S(1)} %get-tuple-element.51), channel_id=1, source_target_pairs={{0,2},{2,4},{4,6},{6,8},{8,10},{10,12},{12,14},{1,3},{3,5},{5,7},{... | collective-permute-start | bytes 393224 | tf_op jit(solution)/shard_map/ppermute | solution.py:16
  106.4 4.4 %collective-permute-done.20 = f32[2,1,64,256]{3,2,1,0:T(8,128)S(1)} collective-permute-done((f32[2,1,64,256]{3,2,1,0:T(8,128)S(1)}, f32[2,1,64,256]{3,2,1,0:T(8,128)S(1)}, u32[]{:S(2)}, u32[]{:S(2)}) %collective-permute-start.20) | collective-permute-done | bytes 131104 | tf_op jit(solution)/shard_map/ppermute | solution.py:19
  116.8 4.0 %collective-permute-start.25 = (f32[2,1,64,256]{3,2,1,0:T(8,128)S(1)}, f32[2,1,64,256]{3,2,1,0:T(8,128)S(1)}, u32[]{:S(2)}, u32[]{:S(2)}) collective-permute-start(f32[2,1,64,256]{3,2,1,0:T(8,128)S(1)} %get-tuple-element.49), channel_id=1, source_target_pairs={{0,2},{2,4},{4,6},{6,8},{8,10},{10,12},{12,14},{1,3},{3,5},{5,7},{... | collective-permute-start | bytes 393224 | tf_op jit(solution)/shard_map/ppermute | solution.py:16
  124.0 4.1 %collective-permute-done.24 = f32[2,1,64,256]{3,2,1,0:T(8,128)S(1)} collective-permute-done((f32[2,1,64,256]{3,2,1,0:T(8,128)S(1)}, f32[2,1,64,256]{3,2,1,0:T(8,128)S(1)}, u32[]{:S(2)}, u32[]{:S(2)}) %collective-permute-start.24) | collective-permute-done | bytes 131104 | tf_op jit(solution)/shard_map/ppermute | solution.py:19
  134.1 3.8 %collective-permute-start.29 = (f32[2,1,64,256]{3,2,1,0:T(8,128)S(1)}, f32[2,1,64,256]{3,2,1,0:T(8,128)S(1)}, u32[]{:S(2)}, u32[]{:S(2)}) collective-permute-start(f32[2,1,64,256]{3,2,1,0:T(8,128)S(1)} %get-tuple-element.47), channel_id=1, source_target_pairs={{0,2},{2,4},{4,6},{6,8},{8,10},{10,12},{12,14},{1,3},{3,5},{5,7},{... | collective-permute-start | bytes 393224 | tf_op jit(solution)/shard_map/ppermute | solution.py:16
  141.1 4.1 %collective-permute-done.28 = f32[2,1,64,256]{3,2,1,0:T(8,128)S(1)} collective-permute-done((f32[2,1,64,256]{3,2,1,0:T(8,128)S(1)}, f32[2,1,64,256]{3,2,1,0:T(8,128)S(1)}, u32[]{:S(2)}, u32[]{:S(2)}) %collective-permute-start.28) | collective-permute-done | bytes 131104 | tf_op jit(solution)/shard_map/ppermute | solution.py:19
  146.6 3.0 %collective-permute-start.31 = (f32[2,6,1,256]{3,2,1,0:T(1,128)S(1)}, f32[2,6,1,256]{3,2,1,0:T(1,128)S(1)}, u32[]{:S(2)}, u32[]{:S(2)}) collective-permute-start(f32[2,6,1,256]{3,2,1,0:T(1,128)S(1)} %get-tuple-element.32), channel_id=1, source_target_pairs={{0,1},{2,3},{4,5},{6,7},{8,9},{10,11},{12,13},{14,15},{16,17},{18,... | collective-permute-start | bytes 36872 | tf_op jit(solution)/shard_map/ppermute | solution.py:16
  153.7 32.3 %psum.15 = f32[]{:T(128)} all-reduce(f32[]{:T(128)} %get-tuple-element.5), channel_id=1, replica_groups=mesh['starts'=2,'gx'=8,'gy'=2] {'gx','gy'}, use_global_device_ids=true, to_apply=%region_6.7 | all-reduce | flops 1 | bytes 8 | tf_op jit(solution)/shard_map/psum | solution.py:87
  186.7 36.6 %all-reduce.10.cloned.1.call-done = f32[2,32,256]{2,1,0:T(8,128)} async-done(((f32[2,32,256]{2,1,0:T(8,128)}), f32[2,32,256]{2,1,0:T(8,128)}) %all-reduce.10.cloned.1.call-update) | async-done | bytes 65552 | tf_op jit(solution)/shard_map/psum | solution.py:88
  (120 shorter events, 61.6 us)
Async XLA Ops:
  7.2 216.1 %all-reduce.10.cloned.1.call-start = ((), (), s32[]{:S(2)}) async-start(), calls=%async_computation | async-start | bytes 131072 | tf_op jit(solution)/shard_map/psum | solution.py:88
  8.3 11.4 %collective-permute-start = (f32[2,1,64,256]{3,2,1,0:T(8,128)S(1)}, f32[2,1,64,256]{3,2,1,0:T(8,128)S(1)}, u32[]{:S(2)}, u32[]{:S(2)}) collective-permute-start(f32[2,1,64,256]{3,2,1,0:T(8,128)S(1)} %get-tuple-element.61), channel_id=1, source_target_pairs={{2,0},{4,2},{6,4},{8,6},{10,8},{12,10},{14,12},{3,1},{5,3},{7,5},{... | collective-permute-start | bytes 393224 | tf_op jit(solution)/shard_map/ppermute | solution.py:19
  9.6 10.0 %collective-permute-start.1 = (f32[2,1,64,256]{3,2,1,0:T(8,128)S(1)}, f32[2,1,64,256]{3,2,1,0:T(8,128)S(1)}, u32[]{:S(2)}, u32[]{:S(2)}) collective-permute-start(f32[2,1,64,256]{3,2,1,0:T(8,128)S(1)} %get-tuple-element.62), channel_id=1, source_target_pairs={{0,2},{2,4},{4,6},{6,8},{8,10},{10,12},{12,14},{1,3},{3,5},{5,7},{... | collective-permute-start | bytes 393224 | tf_op jit(solution)/shard_map/ppermute | solution.py:16
  19.7 4.5 %collective-permute-start.2 = (f32[2,6,1,256]{3,2,1,0:T(1,128)S(1)}, f32[2,6,1,256]{3,2,1,0:T(1,128)S(1)}, u32[]{:S(2)}, u32[]{:S(2)}) collective-permute-start(f32[2,6,1,256]{3,2,1,0:T(1,128)S(1)} %get-tuple-element.45), channel_id=1, source_target_pairs={{1,0},{3,2},{5,4},{7,6},{9,8},{11,10},{13,12},{15,14},{17,16},{19,... | collective-permute-start | bytes 36872 | tf_op jit(solution)/shard_map/ppermute | solution.py:19
  25.7 7.6 %collective-permute-start.5 = (f32[2,1,64,256]{3,2,1,0:T(8,128)S(1)}, f32[2,1,64,256]{3,2,1,0:T(8,128)S(1)}, u32[]{:S(2)}, u32[]{:S(2)}) collective-permute-start(f32[2,1,64,256]{3,2,1,0:T(8,128)S(1)} %get-tuple-element.59), channel_id=1, source_target_pairs={{0,2},{2,4},{4,6},{6,8},{8,10},{10,12},{12,14},{1,3},{3,5},{5,7},{... | collective-permute-start | bytes 393224 | tf_op jit(solution)/shard_map/ppermute | solution.py:16
  30.1 7.4 %collective-permute-start.4 = (f32[2,1,64,256]{3,2,1,0:T(8,128)S(1)}, f32[2,1,64,256]{3,2,1,0:T(8,128)S(1)}, u32[]{:S(2)}, u32[]{:S(2)}) collective-permute-start(f32[2,1,64,256]{3,2,1,0:T(8,128)S(1)} %get-tuple-element.60), channel_id=1, source_target_pairs={{2,0},{4,2},{6,4},{8,6},{10,8},{12,10},{14,12},{3,1},{5,3},{7,5},{... | collective-permute-start | bytes 393224 | tf_op jit(solution)/shard_map/ppermute | solution.py:19
  37.5 4.3 %collective-permute-start.6 = (f32[2,6,1,256]{3,2,1,0:T(1,128)S(1)}, f32[2,6,1,256]{3,2,1,0:T(1,128)S(1)}, u32[]{:S(2)}, u32[]{:S(2)}) collective-permute-start(f32[2,6,1,256]{3,2,1,0:T(1,128)S(1)} %get-tuple-element.43), channel_id=1, source_target_pairs={{1,0},{3,2},{5,4},{7,6},{9,8},{11,10},{13,12},{15,14},{17,16},{19,... | collective-permute-start | bytes 36872 | tf_op jit(solution)/shard_map/ppermute | solution.py:19
  43.3 7.8 %collective-permute-start.9 = (f32[2,1,64,256]{3,2,1,0:T(8,128)S(1)}, f32[2,1,64,256]{3,2,1,0:T(8,128)S(1)}, u32[]{:S(2)}, u32[]{:S(2)}) collective-permute-start(f32[2,1,64,256]{3,2,1,0:T(8,128)S(1)} %get-tuple-element.57), channel_id=1, source_target_pairs={{0,2},{2,4},{4,6},{6,8},{8,10},{10,12},{12,14},{1,3},{3,5},{5,7},{... | collective-permute-start | bytes 393224 | tf_op jit(solution)/shard_map/ppermute | solution.py:16
  47.9 7.4 %collective-permute-start.8 = (f32[2,1,64,256]{3,2,1,0:T(8,128)S(1)}, f32[2,1,64,256]{3,2,1,0:T(8,128)S(1)}, u32[]{:S(2)}, u32[]{:S(2)}) collective-permute-start(f32[2,1,64,256]{3,2,1,0:T(8,128)S(1)} %get-tuple-element.58), channel_id=1, source_target_pairs={{2,0},{4,2},{6,4},{8,6},{10,8},{12,10},{14,12},{3,1},{5,3},{7,5},{... | collective-permute-start | bytes 393224 | tf_op jit(solution)/shard_map/ppermute | solution.py:19
  61.0 7.2 %collective-permute-start.13 = (f32[2,1,64,256]{3,2,1,0:T(8,128)S(1)}, f32[2,1,64,256]{3,2,1,0:T(8,128)S(1)}, u32[]{:S(2)}, u32[]{:S(2)}) collective-permute-start(f32[2,1,64,256]{3,2,1,0:T(8,128)S(1)} %get-tuple-element.55), channel_id=1, source_target_pairs={{0,2},{2,4},{4,6},{6,8},{8,10},{10,12},{12,14},{1,3},{3,5},{5,7},{... | collective-permute-start | bytes 393224 | tf_op jit(solution)/shard_map/ppermute | solution.py:16
  65.0 7.4 %collective-permute-start.12 = (f32[2,1,64,256]{3,2,1,0:T(8,128)S(1)}, f32[2,1,64,256]{3,2,1,0:T(8,128)S(1)}, u32[]{:S(2)}, u32[]{:S(2)}) collective-permute-start(f32[2,1,64,256]{3,2,1,0:T(8,128)S(1)} %get-tuple-element.56), channel_id=1, source_target_pairs={{2,0},{4,2},{6,4},{8,6},{10,8},{12,10},{14,12},{3,1},{5,3},{7,5},{... | collective-permute-start | bytes 393224 | tf_op jit(solution)/shard_map/ppermute | solution.py:19
  72.4 4.3 %collective-permute-start.14 = (f32[2,6,1,256]{3,2,1,0:T(1,128)S(1)}, f32[2,6,1,256]{3,2,1,0:T(1,128)S(1)}, u32[]{:S(2)}, u32[]{:S(2)}) collective-permute-start(f32[2,6,1,256]{3,2,1,0:T(1,128)S(1)} %get-tuple-element.39), channel_id=1, source_target_pairs={{1,0},{3,2},{5,4},{7,6},{9,8},{11,10},{13,12},{15,14},{17,16},{19,... | collective-permute-start | bytes 36872 | tf_op jit(solution)/shard_map/ppermute | solution.py:19
  78.2 7.2 %collective-permute-start.17 = (f32[2,1,64,256]{3,2,1,0:T(8,128)S(1)}, f32[2,1,64,256]{3,2,1,0:T(8,128)S(1)}, u32[]{:S(2)}, u32[]{:S(2)}) collective-permute-start(f32[2,1,64,256]{3,2,1,0:T(8,128)S(1)} %get-tuple-element.53), channel_id=1, source_target_pairs={{0,2},{2,4},{4,6},{6,8},{8,10},{10,12},{12,14},{1,3},{3,5},{5,7},{... | collective-permute-start | bytes 393224 | tf_op jit(solution)/shard_map/ppermute | solution.py:16
  82.3 7.4 %collective-permute-start.16 = (f32[2,1,64,256]{3,2,1,0:T(8,128)S(1)}, f32[2,1,64,256]{3,2,1,0:T(8,128)S(1)}, u32[]{:S(2)}, u32[]{:S(2)}) collective-permute-start(f32[2,1,64,256]{3,2,1,0:T(8,128)S(1)} %get-tuple-element.54), channel_id=1, source_target_pairs={{2,0},{4,2},{6,4},{8,6},{10,8},{12,10},{14,12},{3,1},{5,3},{7,5},{... | collective-permute-start | bytes 393224 | tf_op jit(solution)/shard_map/ppermute | solution.py:19
  90.3 7.7 %collective-permute-start.18 = (f32[2,6,1,256]{3,2,1,0:T(1,128)}, f32[2,6,1,256]{3,2,1,0:T(1,128)}, u32[]{:S(2)}, u32[]{:S(2)}) collective-permute-start(f32[2,6,1,256]{3,2,1,0:T(1,128)} %get-tuple-element.37), channel_id=1, source_target_pairs={{1,0},{3,2},{5,4},{7,6},{9,8},{11,10},{13,12},{15,14},{17,16},{19,... | collective-permute-start | bytes 36872 | tf_op jit(solution)/shard_map/ppermute | solution.py:19
  91.6 6.4 %collective-permute-start.19 = (f32[2,6,1,256]{3,2,1,0:T(1,128)S(1)}, f32[2,6,1,256]{3,2,1,0:T(1,128)}, u32[]{:S(2)}, u32[]{:S(2)}) collective-permute-start(f32[2,6,1,256]{3,2,1,0:T(1,128)S(1)} %get-tuple-element.38), channel_id=1, source_target_pairs={{0,1},{2,3},{4,5},{6,7},{8,9},{10,11},{12,13},{14,15},{16,17},{18,... | collective-permute-start | bytes 36872 | tf_op jit(solution)/shard_map/ppermute | solution.py:16
  100.0 6.5 %collective-permute-start.21 = (f32[2,1,64,256]{3,2,1,0:T(8,128)S(1)}, f32[2,1,64,256]{3,2,1,0:T(8,128)S(1)}, u32[]{:S(2)}, u32[]{:S(2)}) collective-permute-start(f32[2,1,64,256]{3,2,1,0:T(8,128)S(1)} %get-tuple-element.51), channel_id=1, source_target_pairs={{0,2},{2,4},{4,6},{6,8},{8,10},{10,12},{12,14},{1,3},{3,5},{5,7},{... | collective-permute-start | bytes 393224 | tf_op jit(solution)/shard_map/ppermute | solution.py:16
  103.9 6.9 %collective-permute-start.20 = (f32[2,1,64,256]{3,2,1,0:T(8,128)S(1)}, f32[2,1,64,256]{3,2,1,0:T(8,128)S(1)}, u32[]{:S(2)}, u32[]{:S(2)}) collective-permute-start(f32[2,1,64,256]{3,2,1,0:T(8,128)S(1)} %get-tuple-element.52), channel_id=1, source_target_pairs={{2,0},{4,2},{6,4},{8,6},{10,8},{12,10},{14,12},{3,1},{5,3},{7,5},{... | collective-permute-start | bytes 393224 | tf_op jit(solution)/shard_map/ppermute | solution.py:19
  110.8 4.3 %collective-permute-start.22 = (f32[2,6,1,256]{3,2,1,0:T(1,128)S(1)}, f32[2,6,1,256]{3,2,1,0:T(1,128)S(1)}, u32[]{:S(2)}, u32[]{:S(2)}) collective-permute-start(f32[2,6,1,256]{3,2,1,0:T(1,128)S(1)} %get-tuple-element.35), channel_id=1, source_target_pairs={{1,0},{3,2},{5,4},{7,6},{9,8},{11,10},{13,12},{15,14},{17,16},{19,... | collective-permute-start | bytes 36872 | tf_op jit(solution)/shard_map/ppermute | solution.py:19
  116.8 7.2 %collective-permute-start.25 = (f32[2,1,64,256]{3,2,1,0:T(8,128)S(1)}, f32[2,1,64,256]{3,2,1,0:T(8,128)S(1)}, u32[]{:S(2)}, u32[]{:S(2)}) collective-permute-start(f32[2,1,64,256]{3,2,1,0:T(8,128)S(1)} %get-tuple-element.49), channel_id=1, source_target_pairs={{0,2},{2,4},{4,6},{6,8},{8,10},{10,12},{12,14},{1,3},{3,5},{5,7},{... | collective-permute-start | bytes 393224 | tf_op jit(solution)/shard_map/ppermute | solution.py:16
  120.8 7.4 %collective-permute-start.24 = (f32[2,1,64,256]{3,2,1,0:T(8,128)S(1)}, f32[2,1,64,256]{3,2,1,0:T(8,128)S(1)}, u32[]{:S(2)}, u32[]{:S(2)}) collective-permute-start(f32[2,1,64,256]{3,2,1,0:T(8,128)S(1)} %get-tuple-element.50), channel_id=1, source_target_pairs={{2,0},{4,2},{6,4},{8,6},{10,8},{12,10},{14,12},{3,1},{5,3},{7,5},{... | collective-permute-start | bytes 393224 | tf_op jit(solution)/shard_map/ppermute | solution.py:19
  134.1 7.0 %collective-permute-start.29 = (f32[2,1,64,256]{3,2,1,0:T(8,128)S(1)}, f32[2,1,64,256]{3,2,1,0:T(8,128)S(1)}, u32[]{:S(2)}, u32[]{:S(2)}) collective-permute-start(f32[2,1,64,256]{3,2,1,0:T(8,128)S(1)} %get-tuple-element.47), channel_id=1, source_target_pairs={{0,2},{2,4},{4,6},{6,8},{8,10},{10,12},{12,14},{1,3},{3,5},{5,7},{... | collective-permute-start | bytes 393224 | tf_op jit(solution)/shard_map/ppermute | solution.py:16
  137.9 7.4 %collective-permute-start.28 = (f32[2,1,64,256]{3,2,1,0:T(8,128)S(1)}, f32[2,1,64,256]{3,2,1,0:T(8,128)S(1)}, u32[]{:S(2)}, u32[]{:S(2)}) collective-permute-start(f32[2,1,64,256]{3,2,1,0:T(8,128)S(1)} %get-tuple-element.48), channel_id=1, source_target_pairs={{2,0},{4,2},{6,4},{8,6},{10,8},{12,10},{14,12},{3,1},{5,3},{7,5},{... | collective-permute-start | bytes 393224 | tf_op jit(solution)/shard_map/ppermute | solution.py:19
  145.3 4.3 %collective-permute-start.30 = (f32[2,6,1,256]{3,2,1,0:T(1,128)S(1)}, f32[2,6,1,256]{3,2,1,0:T(1,128)S(1)}, u32[]{:S(2)}, u32[]{:S(2)}) collective-permute-start(f32[2,6,1,256]{3,2,1,0:T(1,128)S(1)} %get-tuple-element.31), channel_id=1, source_target_pairs={{1,0},{3,2},{5,4},{7,6},{9,8},{11,10},{13,12},{15,14},{17,16},{19,... | collective-permute-start | bytes 36872 | tf_op jit(solution)/shard_map/ppermute | solution.py:19
  (18 other events, 69.0 us)
Sparse Core Ops, SparseCore 0:
  153.8 69.3 all-reduce.9
where the time goes:
time: 234 us; the launch traced here: 233 us
  waiting for transfers between devices  87.1 us (37%)
  starting transfers between devices  80.2 us (34%)
  blocking collectives  32.3 us (14%)
  between operations  16.6 us (7%)
  other arithmetic  11 us (5%)
  local copies, waits for them, and re-layouts  5.59 us (2%)
    ppermute x16, starting transfers between devices, extended(): lax.ppermute(lax.slice_in_dim(block, block.shape[dim] - width, None, axis...  59.5 us
    psum x1, waiting for transfers between devices, on_device(): rows_sum = lax.psum(rows, 'gx')  36.6 us
    psum x1, blocking collectives, on_device(): squares = lax.psum(local_sq, ('gx', 'gy'))  32.3 us
    ppermute x16, waiting for transfers between devices, extended(): lax.ppermute(lax.slice_in_dim(block, 0, width, axis=dim), axis, backward)  29.1 us
    ppermute x16, waiting for transfers between devices, extended(): lax.ppermute(lax.slice_in_dim(block, block.shape[dim] - width, None, axis...  21.4 us
    ppermute x16, starting transfers between devices, extended(): lax.ppermute(lax.slice_in_dim(block, 0, width, axis=dim), axis, backward)  20.7 us
  transfers between devices with their start and end apart: 33, of which 23 were waited for; matrix products, arithmetic and copies ran while one was open for 2% of the time, Pallas kernels for 0%

commit v1 on v0

--- a/solution.py
+++ b/solution.py
@@ -85,7 +85,7 @@
     )
     local_sq = jnp.sum(chi_start * chi_start)
     squares = lax.psum(local_sq, ("gx", "gy"))
-    rows_sum = lax.psum(rows, "gx")
+    rows_sum = jnp.sum(lax.all_gather(rows, "gx"), axis=0)
     power = squares / float(total_x * total_y * depth)
     grad_rows = rows_sum / jnp.sqrt(float(total_x) * (power + 1e-06))
     return (chi_start, grad_rows, jnp.reshape(power, (1,)))

time: 234 us -> 215 us (0.919)
  waiting for transfers between devices: 87.1 us -> 50.5 us
  blocking collectives: 32.3 us -> 63.4 us
  between operations: 16.6 us -> 3.17 us
    psum x1 -> x0, waiting for transfers between devices: 36.6 us -> none  [on_device(): rows_sum = lax.psum(rows, 'gx')]
    all_gather x0 -> x1, blocking collectives: none -> 31.3 us  [on_device(): rows_sum = jnp.sum(lax.all_gather(rows, 'gx'), axis=0)]
  transfers between devices with their start and end apart: 33 -> 32, of which waited for: 23 -> 22; matrix products, arithmetic and copies ran while one was open for 2% -> 2% of each run, Pallas kernels for 0% -> 0%
where the time goes in v1:
time: 215 us; the launch traced here: 214 us
  starting transfers between devices  80.2 us (37%)
  blocking collectives  63.4 us (29%)
  waiting for transfers between devices  50.5 us (23%)
  other arithmetic  11.6 us (5%)
  local copies, waits for them, and re-layouts  5.06 us (2%)
  between operations  3.17 us (1%)
    ppermute x16, starting transfers between devices, extended(): lax.ppermute(lax.slice_in_dim(block, block.shape[dim] - width, None, axis...  59.5 us
    psum x1, blocking collectives, on_device(): squares = lax.psum(local_sq, ('gx', 'gy'))  32.2 us
    all_gather x1, blocking collectives, on_device(): rows_sum = jnp.sum(lax.all_gather(rows, 'gx'), axis=0)  31.3 us
    ppermute x16, waiting for transfers between devices, extended(): lax.ppermute(lax.slice_in_dim(block, 0, width, axis=dim), axis, backward)  29.1 us
    ppermute x16, waiting for transfers between devices, extended(): lax.ppermute(lax.slice_in_dim(block, block.shape[dim] - width, None, axis...  21.4 us
    ppermute x16, starting transfers between devices, extended(): lax.ppermute(lax.slice_in_dim(block, 0, width, axis=dim), axis, backward)  20.7 us
  transfers between devices with their start and end apart: 32, of which 22 were waited for; matrix products, arithmetic and copies ran while one was open for 2% of the time, Pallas kernels for 0%

profile of v1, /device:TPU:0, one launch (start us, length us, event | category | flops | bytes accessed | tf_op | source)
XLA Modules:
  0.0 214.0 jit_solution(1937929946179994768)
XLA Ops:
  3.0 5.5 %collective-permute-start.1 = (f32[2,1,64,256]{3,2,1,0:T(8,128)S(1)}, f32[2,1,64,256]{3,2,1,0:T(8,128)S(1)}, u32[]{:S(2)}, u32[]{:S(2)}) collective-permute-start(f32[2,1,64,256]{3,2,1,0:T(8,128)S(1)} %get-tuple-element.62), channel_id=1, source_target_pairs={{0,2},{2,4},{4,6},{6,8},{8,10},{10,12},{12,14},{1,3},{3,5},{5,7},{... | collective-permute-start | bytes 393224 | tf_op jit(solution)/shard_map/ppermute | solution.py:16
  9.9 3.1 %collective-permute-done.1 = f32[2,1,64,256]{3,2,1,0:T(8,128)S(1)} collective-permute-done((f32[2,1,64,256]{3,2,1,0:T(8,128)S(1)}, f32[2,1,64,256]{3,2,1,0:T(8,128)S(1)}, u32[]{:S(2)}, u32[]{:S(2)}) %collective-permute-start.1) | collective-permute-done | bytes 131104 | tf_op jit(solution)/shard_map/ppermute | solution.py:16
  14.4 3.0 %collective-permute-start.3 = (f32[2,6,1,256]{3,2,1,0:T(1,128)S(1)}, f32[2,6,1,256]{3,2,1,0:T(1,128)S(1)}, u32[]{:S(2)}, u32[]{:S(2)}) collective-permute-start(f32[2,6,1,256]{3,2,1,0:T(1,128)S(1)} %get-tuple-element.46), channel_id=1, source_target_pairs={{0,1},{2,3},{4,5},{6,7},{8,9},{10,11},{12,13},{14,15},{16,17},{18,... | collective-permute-start | bytes 36872 | tf_op jit(solution)/shard_map/ppermute | solution.py:16
  19.2 4.4 %collective-permute-start.5 = (f32[2,1,64,256]{3,2,1,0:T(8,128)S(1)}, f32[2,1,64,256]{3,2,1,0:T(8,128)S(1)}, u32[]{:S(2)}, u32[]{:S(2)}) collective-permute-start(f32[2,1,64,256]{3,2,1,0:T(8,128)S(1)} %get-tuple-element.59), channel_id=1, source_target_pairs={{0,2},{2,4},{4,6},{6,8},{8,10},{10,12},{12,14},{1,3},{3,5},{5,7},{... | collective-permute-start | bytes 393224 | tf_op jit(solution)/shard_map/ppermute | solution.py:16
  26.8 4.1 %collective-permute-done.4 = f32[2,1,64,256]{3,2,1,0:T(8,128)S(1)} collective-permute-done((f32[2,1,64,256]{3,2,1,0:T(8,128)S(1)}, f32[2,1,64,256]{3,2,1,0:T(8,128)S(1)}, u32[]{:S(2)}, u32[]{:S(2)}) %collective-permute-start.4) | collective-permute-done | bytes 131104 | tf_op jit(solution)/shard_map/ppermute | solution.py:19
  32.2 3.0 %collective-permute-start.7 = (f32[2,6,1,256]{3,2,1,0:T(1,128)S(1)}, f32[2,6,1,256]{3,2,1,0:T(1,128)S(1)}, u32[]{:S(2)}, u32[]{:S(2)}) collective-permute-start(f32[2,6,1,256]{3,2,1,0:T(1,128)S(1)} %get-tuple-element.44), channel_id=1, source_target_pairs={{0,1},{2,3},{4,5},{6,7},{8,9},{10,11},{12,13},{14,15},{16,17},{18,... | collective-permute-start | bytes 36872 | tf_op jit(solution)/shard_map/ppermute | solution.py:16
  36.7 4.5 %collective-permute-start.9 = (f32[2,1,64,256]{3,2,1,0:T(8,128)S(1)}, f32[2,1,64,256]{3,2,1,0:T(8,128)S(1)}, u32[]{:S(2)}, u32[]{:S(2)}) collective-permute-start(f32[2,1,64,256]{3,2,1,0:T(8,128)S(1)} %get-tuple-element.57), channel_id=1, source_target_pairs={{0,2},{2,4},{4,6},{6,8},{8,10},{10,12},{12,14},{1,3},{3,5},{5,7},{... | collective-permute-start | bytes 393224 | tf_op jit(solution)/shard_map/ppermute | solution.py:16
  44.5 4.1 %collective-permute-done.8 = f32[2,1,64,256]{3,2,1,0:T(8,128)S(1)} collective-permute-done((f32[2,1,64,256]{3,2,1,0:T(8,128)S(1)}, f32[2,1,64,256]{3,2,1,0:T(8,128)S(1)}, u32[]{:S(2)}, u32[]{:S(2)}) %collective-permute-start.8) | collective-permute-done | bytes 131104 | tf_op jit(solution)/shard_map/ppermute | solution.py:19
  50.0 3.0 %collective-permute-start.11 = (f32[2,6,1,256]{3,2,1,0:T(1,128)S(1)}, f32[2,6,1,256]{3,2,1,0:T(1,128)S(1)}, u32[]{:S(2)}, u32[]{:S(2)}) collective-permute-start(f32[2,6,1,256]{3,2,1,0:T(1,128)S(1)} %get-tuple-element.42), channel_id=1, source_target_pairs={{0,1},{2,3},{4,5},{6,7},{8,9},{10,11},{12,13},{14,15},{16,17},{18,... | collective-permute-start | bytes 36872 | tf_op jit(solution)/shard_map/ppermute | solution.py:16
  54.4 4.0 %collective-permute-start.13 = (f32[2,1,64,256]{3,2,1,0:T(8,128)S(1)}, f32[2,1,64,256]{3,2,1,0:T(8,128)S(1)}, u32[]{:S(2)}, u32[]{:S(2)}) collective-permute-start(f32[2,1,64,256]{3,2,1,0:T(8,128)S(1)} %get-tuple-element.55), channel_id=1, source_target_pairs={{0,2},{2,4},{4,6},{6,8},{8,10},{10,12},{12,14},{1,3},{3,5},{5,7},{... | collective-permute-start | bytes 393224 | tf_op jit(solution)/shard_map/ppermute | solution.py:16
  61.7 4.1 %collective-permute-done.12 = f32[2,1,64,256]{3,2,1,0:T(8,128)S(1)} collective-permute-done((f32[2,1,64,256]{3,2,1,0:T(8,128)S(1)}, f32[2,1,64,256]{3,2,1,0:T(8,128)S(1)}, u32[]{:S(2)}, u32[]{:S(2)}) %collective-permute-start.12) | collective-permute-done | bytes 131104 | tf_op jit(solution)/shard_map/ppermute | solution.py:19
  67.1 3.0 %collective-permute-start.15 = (f32[2,6,1,256]{3,2,1,0:T(1,128)S(1)}, f32[2,6,1,256]{3,2,1,0:T(1,128)S(1)}, u32[]{:S(2)}, u32[]{:S(2)}) collective-permute-start(f32[2,6,1,256]{3,2,1,0:T(1,128)S(1)} %get-tuple-element.40), channel_id=1, source_target_pairs={{0,1},{2,3},{4,5},{6,7},{8,9},{10,11},{12,13},{14,15},{16,17},{18,... | collective-permute-start | bytes 36872 | tf_op jit(solution)/shard_map/ppermute | solution.py:16
  71.7 4.0 %collective-permute-start.17 = (f32[2,1,64,256]{3,2,1,0:T(8,128)S(1)}, f32[2,1,64,256]{3,2,1,0:T(8,128)S(1)}, u32[]{:S(2)}, u32[]{:S(2)}) collective-permute-start(f32[2,1,64,256]{3,2,1,0:T(8,128)S(1)} %get-tuple-element.53), channel_id=1, source_target_pairs={{0,2},{2,4},{4,6},{6,8},{8,10},{10,12},{12,14},{1,3},{3,5},{5,7},{... | collective-permute-start | bytes 393224 | tf_op jit(solution)/shard_map/ppermute | solution.py:16
  78.9 4.1 %collective-permute-done.16 = f32[2,1,64,256]{3,2,1,0:T(8,128)S(1)} collective-permute-done((f32[2,1,64,256]{3,2,1,0:T(8,128)S(1)}, f32[2,1,64,256]{3,2,1,0:T(8,128)S(1)}, u32[]{:S(2)}, u32[]{:S(2)}) %collective-permute-start.16) | collective-permute-done | bytes 131104 | tf_op jit(solution)/shard_map/ppermute | solution.py:19
  85.0 4.2 %collective-permute-start.19 = (f32[2,6,1,256]{3,2,1,0:T(1,128)S(1)}, f32[2,6,1,256]{3,2,1,0:T(1,128)}, u32[]{:S(2)}, u32[]{:S(2)}) collective-permute-start(f32[2,6,1,256]{3,2,1,0:T(1,128)S(1)} %get-tuple-element.38), channel_id=1, source_target_pairs={{0,1},{2,3},{4,5},{6,7},{8,9},{10,11},{12,13},{14,15},{16,17},{18,... | collective-permute-start | bytes 36872 | tf_op jit(solution)/shard_map/ppermute | solution.py:16
  93.4 4.0 %collective-permute-start.21 = (f32[2,1,64,256]{3,2,1,0:T(8,128)S(1)}, f32[2,1,64,256]{3,2,1,0:T(8,128)S(1)}, u32[]{:S(2)}, u32[]{:S(2)}) collective-permute-start(f32[2,1,64,256]{3,2,1,0:T(8,128)S(1)} %get-tuple-element.51), channel_id=1, source_target_pairs={{0,2},{2,4},{4,6},{6,8},{8,10},{10,12},{12,14},{1,3},{3,5},{5,7},{... | collective-permute-start | bytes 393224 | tf_op jit(solution)/shard_map/ppermute | solution.py:16
  99.9 4.4 %collective-permute-done.20 = f32[2,1,64,256]{3,2,1,0:T(8,128)S(1)} collective-permute-done((f32[2,1,64,256]{3,2,1,0:T(8,128)S(1)}, f32[2,1,64,256]{3,2,1,0:T(8,128)S(1)}, u32[]{:S(2)}, u32[]{:S(2)}) %collective-permute-start.20) | collective-permute-done | bytes 131104 | tf_op jit(solution)/shard_map/ppermute | solution.py:19
  110.2 4.0 %collective-permute-start.25 = (f32[2,1,64,256]{3,2,1,0:T(8,128)S(1)}, f32[2,1,64,256]{3,2,1,0:T(8,128)S(1)}, u32[]{:S(2)}, u32[]{:S(2)}) collective-permute-start(f32[2,1,64,256]{3,2,1,0:T(8,128)S(1)} %get-tuple-element.49), channel_id=1, source_target_pairs={{0,2},{2,4},{4,6},{6,8},{8,10},{10,12},{12,14},{1,3},{3,5},{5,7},{... | collective-permute-start | bytes 393224 | tf_op jit(solution)/shard_map/ppermute | solution.py:16
  117.4 4.1 %collective-permute-done.24 = f32[2,1,64,256]{3,2,1,0:T(8,128)S(1)} collective-permute-done((f32[2,1,64,256]{3,2,1,0:T(8,128)S(1)}, f32[2,1,64,256]{3,2,1,0:T(8,128)S(1)}, u32[]{:S(2)}, u32[]{:S(2)}) %collective-permute-start.24) | collective-permute-done | bytes 131104 | tf_op jit(solution)/shard_map/ppermute | solution.py:19
  122.9 3.0 %collective-permute-start.27 = (f32[2,6,1,256]{3,2,1,0:T(1,128)S(1)}, f32[2,6,1,256]{3,2,1,0:T(1,128)S(1)}, u32[]{:S(2)}, u32[]{:S(2)}) collective-permute-start(f32[2,6,1,256]{3,2,1,0:T(1,128)S(1)} %get-tuple-element.34), channel_id=1, source_target_pairs={{0,1},{2,3},{4,5},{6,7},{8,9},{10,11},{12,13},{14,15},{16,17},{18,... | collective-permute-start | bytes 36872 | tf_op jit(solution)/shard_map/ppermute | solution.py:16
  127.5 3.8 %collective-permute-start.29 = (f32[2,1,64,256]{3,2,1,0:T(8,128)S(1)}, f32[2,1,64,256]{3,2,1,0:T(8,128)S(1)}, u32[]{:S(2)}, u32[]{:S(2)}) collective-permute-start(f32[2,1,64,256]{3,2,1,0:T(8,128)S(1)} %get-tuple-element.47), channel_id=1, source_target_pairs={{0,2},{2,4},{4,6},{6,8},{8,10},{10,12},{12,14},{1,3},{3,5},{5,7},{... | collective-permute-start | bytes 393224 | tf_op jit(solution)/shard_map/ppermute | solution.py:16
  134.5 4.1 %collective-permute-done.28 = f32[2,1,64,256]{3,2,1,0:T(8,128)S(1)} collective-permute-done((f32[2,1,64,256]{3,2,1,0:T(8,128)S(1)}, f32[2,1,64,256]{3,2,1,0:T(8,128)S(1)}, u32[]{:S(2)}, u32[]{:S(2)}) %collective-permute-start.28) | collective-permute-done | bytes 131104 | tf_op jit(solution)/shard_map/ppermute | solution.py:19
  146.2 32.2 %psum.7 = f32[]{:T(128)} all-reduce(f32[]{:T(128)} %get-tuple-element.5), channel_id=1, replica_groups=mesh['starts'=2,'gx'=8,'gy'=2] {'gx','gy'}, use_global_device_ids=true, to_apply=%region_6.7 | all-reduce | flops 1 | bytes 8 | tf_op jit(solution)/shard_map/psum | solution.py:87
  180.9 31.3 %all-gather = f32[16,32,256]{2,1,0:T(8,128)S(1)} all-gather(f32[2,32,256]{2,1,0:T(8,128)S(1)} %pad_maximum_fusion.66), channel_id=2, replica_groups=mesh['starts'=2,'gx'=8,'gy'=2] {'gx'}, dimensions={0}, use_global_device_ids=true | all-gather | bytes 589824 | tf_op jit(solution)/shard_map/all_gather | solution.py:88
  (115 shorter events, 61.7 us)
Async XLA Ops:
  1.7 11.4 %collective-permute-start = (f32[2,1,64,256]{3,2,1,0:T(8,128)S(1)}, f32[2,1,64,256]{3,2,1,0:T(8,128)S(1)}, u32[]{:S(2)}, u32[]{:S(2)}) collective-permute-start(f32[2,1,64,256]{3,2,1,0:T(8,128)S(1)} %get-tuple-element.61), channel_id=1, source_target_pairs={{2,0},{4,2},{6,4},{8,6},{10,8},{12,10},{14,12},{3,1},{5,3},{7,5},{... | collective-permute-start | bytes 393224 | tf_op jit(solution)/shard_map/ppermute | solution.py:19
  3.0 10.0 %collective-permute-start.1 = (f32[2,1,64,256]{3,2,1,0:T(8,128)S(1)}, f32[2,1,64,256]{3,2,1,0:T(8,128)S(1)}, u32[]{:S(2)}, u32[]{:S(2)}) collective-permute-start(f32[2,1,64,256]{3,2,1,0:T(8,128)S(1)} %get-tuple-element.62), channel_id=1, source_target_pairs={{0,2},{2,4},{4,6},{6,8},{8,10},{10,12},{12,14},{1,3},{3,5},{5,7},{... | collective-permute-start | bytes 393224 | tf_op jit(solution)/shard_map/ppermute | solution.py:16
  13.1 4.5 %collective-permute-start.2 = (f32[2,6,1,256]{3,2,1,0:T(1,128)S(1)}, f32[2,6,1,256]{3,2,1,0:T(1,128)S(1)}, u32[]{:S(2)}, u32[]{:S(2)}) collective-permute-start(f32[2,6,1,256]{3,2,1,0:T(1,128)S(1)} %get-tuple-element.45), channel_id=1, source_target_pairs={{1,0},{3,2},{5,4},{7,6},{9,8},{11,10},{13,12},{15,14},{17,16},{19,... | collective-permute-start | bytes 36872 | tf_op jit(solution)/shard_map/ppermute | solution.py:19
  19.2 7.6 %collective-permute-start.5 = (f32[2,1,64,256]{3,2,1,0:T(8,128)S(1)}, f32[2,1,64,256]{3,2,1,0:T(8,128)S(1)}, u32[]{:S(2)}, u32[]{:S(2)}) collective-permute-start(f32[2,1,64,256]{3,2,1,0:T(8,128)S(1)} %get-tuple-element.59), channel_id=1, source_target_pairs={{0,2},{2,4},{4,6},{6,8},{8,10},{10,12},{12,14},{1,3},{3,5},{5,7},{... | collective-permute-start | bytes 393224 | tf_op jit(solution)/shard_map/ppermute | solution.py:16
  23.6 7.4 %collective-permute-start.4 = (f32[2,1,64,256]{3,2,1,0:T(8,128)S(1)}, f32[2,1,64,256]{3,2,1,0:T(8,128)S(1)}, u32[]{:S(2)}, u32[]{:S(2)}) collective-permute-start(f32[2,1,64,256]{3,2,1,0:T(8,128)S(1)} %get-tuple-element.60), channel_id=1, source_target_pairs={{2,0},{4,2},{6,4},{8,6},{10,8},{12,10},{14,12},{3,1},{5,3},{7,5},{... | collective-permute-start | bytes 393224 | tf_op jit(solution)/shard_map/ppermute | solution.py:19
  30.9 4.3 %collective-permute-start.6 = (f32[2,6,1,256]{3,2,1,0:T(1,128)S(1)}, f32[2,6,1,256]{3,2,1,0:T(1,128)S(1)}, u32[]{:S(2)}, u32[]{:S(2)}) collective-permute-start(f32[2,6,1,256]{3,2,1,0:T(1,128)S(1)} %get-tuple-element.43), channel_id=1, source_target_pairs={{1,0},{3,2},{5,4},{7,6},{9,8},{11,10},{13,12},{15,14},{17,16},{19,... | collective-permute-start | bytes 36872 | tf_op jit(solution)/shard_map/ppermute | solution.py:19
  36.7 7.8 %collective-permute-start.9 = (f32[2,1,64,256]{3,2,1,0:T(8,128)S(1)}, f32[2,1,64,256]{3,2,1,0:T(8,128)S(1)}, u32[]{:S(2)}, u32[]{:S(2)}) collective-permute-start(f32[2,1,64,256]{3,2,1,0:T(8,128)S(1)} %get-tuple-element.57), channel_id=1, source_target_pairs={{0,2},{2,4},{4,6},{6,8},{8,10},{10,12},{12,14},{1,3},{3,5},{5,7},{... | collective-permute-start | bytes 393224 | tf_op jit(solution)/shard_map/ppermute | solution.py:16
  41.3 7.4 %collective-permute-start.8 = (f32[2,1,64,256]{3,2,1,0:T(8,128)S(1)}, f32[2,1,64,256]{3,2,1,0:T(8,128)S(1)}, u32[]{:S(2)}, u32[]{:S(2)}) collective-permute-start(f32[2,1,64,256]{3,2,1,0:T(8,128)S(1)} %get-tuple-element.58), channel_id=1, source_target_pairs={{2,0},{4,2},{6,4},{8,6},{10,8},{12,10},{14,12},{3,1},{5,3},{7,5},{... | collective-permute-start | bytes 393224 | tf_op jit(solution)/shard_map/ppermute | solution.py:19
  48.7 4.3 %collective-permute-start.10 = (f32[2,6,1,256]{3,2,1,0:T(1,128)S(1)}, f32[2,6,1,256]{3,2,1,0:T(1,128)S(1)}, u32[]{:S(2)}, u32[]{:S(2)}) collective-permute-start(f32[2,6,1,256]{3,2,1,0:T(1,128)S(1)} %get-tuple-element.41), channel_id=1, source_target_pairs={{1,0},{3,2},{5,4},{7,6},{9,8},{11,10},{13,12},{15,14},{17,16},{19,... | collective-permute-start | bytes 36872 | tf_op jit(solution)/shard_map/ppermute | solution.py:19
  54.4 7.2 %collective-permute-start.13 = (f32[2,1,64,256]{3,2,1,0:T(8,128)S(1)}, f32[2,1,64,256]{3,2,1,0:T(8,128)S(1)}, u32[]{:S(2)}, u32[]{:S(2)}) collective-permute-start(f32[2,1,64,256]{3,2,1,0:T(8,128)S(1)} %get-tuple-element.55), channel_id=1, source_target_pairs={{0,2},{2,4},{4,6},{6,8},{8,10},{10,12},{12,14},{1,3},{3,5},{5,7},{... | collective-permute-start | bytes 393224 | tf_op jit(solution)/shard_map/ppermute | solution.py:16
  58.4 7.4 %collective-permute-start.12 = (f32[2,1,64,256]{3,2,1,0:T(8,128)S(1)}, f32[2,1,64,256]{3,2,1,0:T(8,128)S(1)}, u32[]{:S(2)}, u32[]{:S(2)}) collective-permute-start(f32[2,1,64,256]{3,2,1,0:T(8,128)S(1)} %get-tuple-element.56), channel_id=1, source_target_pairs={{2,0},{4,2},{6,4},{8,6},{10,8},{12,10},{14,12},{3,1},{5,3},{7,5},{... | collective-permute-start | bytes 393224 | tf_op jit(solution)/shard_map/ppermute | solution.py:19
  65.8 4.3 %collective-permute-start.14 = (f32[2,6,1,256]{3,2,1,0:T(1,128)S(1)}, f32[2,6,1,256]{3,2,1,0:T(1,128)S(1)}, u32[]{:S(2)}, u32[]{:S(2)}) collective-permute-start(f32[2,6,1,256]{3,2,1,0:T(1,128)S(1)} %get-tuple-element.39), channel_id=1, source_target_pairs={{1,0},{3,2},{5,4},{7,6},{9,8},{11,10},{13,12},{15,14},{17,16},{19,... | collective-permute-start | bytes 36872 | tf_op jit(solution)/shard_map/ppermute | solution.py:19
  71.7 7.2 %collective-permute-start.17 = (f32[2,1,64,256]{3,2,1,0:T(8,128)S(1)}, f32[2,1,64,256]{3,2,1,0:T(8,128)S(1)}, u32[]{:S(2)}, u32[]{:S(2)}) collective-permute-start(f32[2,1,64,256]{3,2,1,0:T(8,128)S(1)} %get-tuple-element.53), channel_id=1, source_target_pairs={{0,2},{2,4},{4,6},{6,8},{8,10},{10,12},{12,14},{1,3},{3,5},{5,7},{... | collective-permute-start | bytes 393224 | tf_op jit(solution)/shard_map/ppermute | solution.py:16
  75.7 7.4 %collective-permute-start.16 = (f32[2,1,64,256]{3,2,1,0:T(8,128)S(1)}, f32[2,1,64,256]{3,2,1,0:T(8,128)S(1)}, u32[]{:S(2)}, u32[]{:S(2)}) collective-permute-start(f32[2,1,64,256]{3,2,1,0:T(8,128)S(1)} %get-tuple-element.54), channel_id=1, source_target_pairs={{2,0},{4,2},{6,4},{8,6},{10,8},{12,10},{14,12},{3,1},{5,3},{7,5},{... | collective-permute-start | bytes 393224 | tf_op jit(solution)/shard_map/ppermute | solution.py:19
  83.7 7.7 %collective-permute-start.18 = (f32[2,6,1,256]{3,2,1,0:T(1,128)}, f32[2,6,1,256]{3,2,1,0:T(1,128)}, u32[]{:S(2)}, u32[]{:S(2)}) collective-permute-start(f32[2,6,1,256]{3,2,1,0:T(1,128)} %get-tuple-element.37), channel_id=1, source_target_pairs={{1,0},{3,2},{5,4},{7,6},{9,8},{11,10},{13,12},{15,14},{17,16},{19,... | collective-permute-start | bytes 36872 | tf_op jit(solution)/shard_map/ppermute | solution.py:19
  85.0 6.4 %collective-permute-start.19 = (f32[2,6,1,256]{3,2,1,0:T(1,128)S(1)}, f32[2,6,1,256]{3,2,1,0:T(1,128)}, u32[]{:S(2)}, u32[]{:S(2)}) collective-permute-start(f32[2,6,1,256]{3,2,1,0:T(1,128)S(1)} %get-tuple-element.38), channel_id=1, source_target_pairs={{0,1},{2,3},{4,5},{6,7},{8,9},{10,11},{12,13},{14,15},{16,17},{18,... | collective-permute-start | bytes 36872 | tf_op jit(solution)/shard_map/ppermute | solution.py:16
  93.4 6.5 %collective-permute-start.21 = (f32[2,1,64,256]{3,2,1,0:T(8,128)S(1)}, f32[2,1,64,256]{3,2,1,0:T(8,128)S(1)}, u32[]{:S(2)}, u32[]{:S(2)}) collective-permute-start(f32[2,1,64,256]{3,2,1,0:T(8,128)S(1)} %get-tuple-element.51), channel_id=1, source_target_pairs={{0,2},{2,4},{4,6},{6,8},{8,10},{10,12},{12,14},{1,3},{3,5},{5,7},{... | collective-permute-start | bytes 393224 | tf_op jit(solution)/shard_map/ppermute | solution.py:16
  97.4 6.9 %collective-permute-start.20 = (f32[2,1,64,256]{3,2,1,0:T(8,128)S(1)}, f32[2,1,64,256]{3,2,1,0:T(8,128)S(1)}, u32[]{:S(2)}, u32[]{:S(2)}) collective-permute-start(f32[2,1,64,256]{3,2,1,0:T(8,128)S(1)} %get-tuple-element.52), channel_id=1, source_target_pairs={{2,0},{4,2},{6,4},{8,6},{10,8},{12,10},{14,12},{3,1},{5,3},{7,5},{... | collective-permute-start | bytes 393224 | tf_op jit(solution)/shard_map/ppermute | solution.py:19
  110.2 7.2 %collective-permute-start.25 = (f32[2,1,64,256]{3,2,1,0:T(8,128)S(1)}, f32[2,1,64,256]{3,2,1,0:T(8,128)S(1)}, u32[]{:S(2)}, u32[]{:S(2)}) collective-permute-start(f32[2,1,64,256]{3,2,1,0:T(8,128)S(1)} %get-tuple-element.49), channel_id=1, source_target_pairs={{0,2},{2,4},{4,6},{6,8},{8,10},{10,12},{12,14},{1,3},{3,5},{5,7},{... | collective-permute-start | bytes 393224 | tf_op jit(solution)/shard_map/ppermute | solution.py:16
  114.2 7.4 %collective-permute-start.24 = (f32[2,1,64,256]{3,2,1,0:T(8,128)S(1)}, f32[2,1,64,256]{3,2,1,0:T(8,128)S(1)}, u32[]{:S(2)}, u32[]{:S(2)}) collective-permute-start(f32[2,1,64,256]{3,2,1,0:T(8,128)S(1)} %get-tuple-element.50), channel_id=1, source_target_pairs={{2,0},{4,2},{6,4},{8,6},{10,8},{12,10},{14,12},{3,1},{5,3},{7,5},{... | collective-permute-start | bytes 393224 | tf_op jit(solution)/shard_map/ppermute | solution.py:19
  121.6 4.3 %collective-permute-start.26 = (f32[2,6,1,256]{3,2,1,0:T(1,128)S(1)}, f32[2,6,1,256]{3,2,1,0:T(1,128)S(1)}, u32[]{:S(2)}, u32[]{:S(2)}) collective-permute-start(f32[2,6,1,256]{3,2,1,0:T(1,128)S(1)} %get-tuple-element.33), channel_id=1, source_target_pairs={{1,0},{3,2},{5,4},{7,6},{9,8},{11,10},{13,12},{15,14},{17,16},{19,... | collective-permute-start | bytes 36872 | tf_op jit(solution)/shard_map/ppermute | solution.py:19
  127.5 7.0 %collective-permute-start.29 = (f32[2,1,64,256]{3,2,1,0:T(8,128)S(1)}, f32[2,1,64,256]{3,2,1,0:T(8,128)S(1)}, u32[]{:S(2)}, u32[]{:S(2)}) collective-permute-start(f32[2,1,64,256]{3,2,1,0:T(8,128)S(1)} %get-tuple-element.47), channel_id=1, source_target_pairs={{0,2},{2,4},{4,6},{6,8},{8,10},{10,12},{12,14},{1,3},{3,5},{5,7},{... | collective-permute-start | bytes 393224 | tf_op jit(solution)/shard_map/ppermute | solution.py:16
  131.3 7.4 %collective-permute-start.28 = (f32[2,1,64,256]{3,2,1,0:T(8,128)S(1)}, f32[2,1,64,256]{3,2,1,0:T(8,128)S(1)}, u32[]{:S(2)}, u32[]{:S(2)}) collective-permute-start(f32[2,1,64,256]{3,2,1,0:T(8,128)S(1)} %get-tuple-element.48), channel_id=1, source_target_pairs={{2,0},{4,2},{6,4},{8,6},{10,8},{12,10},{14,12},{3,1},{5,3},{7,5},{... | collective-permute-start | bytes 393224 | tf_op jit(solution)/shard_map/ppermute | solution.py:19
  138.7 4.3 %collective-permute-start.30 = (f32[2,6,1,256]{3,2,1,0:T(1,128)S(1)}, f32[2,6,1,256]{3,2,1,0:T(1,128)S(1)}, u32[]{:S(2)}, u32[]{:S(2)}) collective-permute-start(f32[2,6,1,256]{3,2,1,0:T(1,128)S(1)} %get-tuple-element.31), channel_id=1, source_target_pairs={{1,0},{3,2},{5,4},{7,6},{9,8},{11,10},{13,12},{15,14},{17,16},{19,... | collective-permute-start | bytes 36872 | tf_op jit(solution)/shard_map/ppermute | solution.py:19
  (15 other events, 62.7 us)
